TPU v7x, 32 devices: a whole 2x2x4 slice. The times are simulated.
32 devices in a mesh: ctx: 4 (over y, core), ep: 8 (over z, x).
Axes of the slice: x: 2, y: 2, z: 4, core: 2. Of those that a mesh axis runs over, the one named last changes fastest.
Arguments:
- tokens: bfloat16 [1024, 3584], P('ep', 'ctx'), may hold values from -6 to 6
- cotangent: bfloat16 [1024, 3584], P('ep', 'ctx'), may hold values from -0.8984375 to 0.8984375
- expert_ids: int32 [1024, 1], P('ep'), may hold values from 0 to 7; in each aligned block of 128 rows (0 to 127, 128 to 255, ...) at most 24 rows name the same one
- route_gates: float32 [1024, 1], P('ep'), may hold values from 0.1 to 1
- w_gate: bfloat16 [8, 3584, 2048], P('ep', None, 'ctx'), may hold values from -0.125 to 0.125
- w_up: bfloat16 [8, 3584, 2048], P('ep', None, 'ctx'), may hold values from -0.09375 to 0.09375
- w_down: bfloat16 [8, 2048, 3584], P('ep', 'ctx'), may hold values from -0.1875 to 0.1875
Outputs:
- layer_out: bfloat16 [1024, 3584], P('ep', 'ctx')
- input_grad: bfloat16 [1024, 3584], P('ep', 'ctx')
- gate_grad: float32 [1024, 1], P('ep')
- w_gate_grad: bfloat16 [8, 3584, 2048], P('ep', None, 'ctx')
- w_up_grad: bfloat16 [8, 3584, 2048], P('ep', None, 'ctx')
Inputs may be any that keep to these rules, and one draw needn't show every extreme that they name: `expert_ids`: within each aligned block of 128 tokens (the tokens of one index of ep) no expert is named more than 24 times, a bound that some block reaches; the routes of one token name different experts.
All inputs are finite; a program needn't handle non-finite values.
Results may differ from a plain program's by a relative error of at most 0.015.
Values may be sent and summed in bfloat16 or wider, within the bound.
No kernel may reach another device: no remote copies, remote signals or barrier semaphores. Data moves between devices by JAX's collectives and lax.ppermute only.
A program may use at most 128 MiB of HBM per device.

v0:
```python
import jax
import jax.numpy as jnp
from jax import lax
from jax.sharding import PartitionSpec as P


def route_tables(expert_ids, experts, capacity):
    tok_rows, routes = expert_ids.shape
    flat_ids = expert_ids.reshape(-1)
    labels = jnp.arange(experts, dtype=jnp.int32)
    onehot = (flat_ids[:, None] == labels[None, :]).astype(jnp.int32)
    earlier = jnp.cumsum(onehot, axis=0) - onehot
    slot_rank = jnp.sum(earlier * onehot, axis=1)
    slot_ids = (flat_ids * capacity + slot_rank).reshape(tok_rows, routes)
    positions = jnp.arange(experts * capacity, dtype=jnp.int32)
    return [slot_ids[:, 0][:, None] == positions[None, :]]


def shards(tokens, cotangent, expert_ids, route_gates, w_gate, w_up, w_down):
    tok_rows, routes = expert_ids.shape
    experts = lax.axis_size("ep")
    capacity = 3 * tok_rows * routes // (2 * experts)
    slot_count = experts * capacity
    col_width = tokens.shape[1]
    route_maps = route_tables(expert_ids, experts, capacity)
    chosen = route_maps[0].astype(jnp.bfloat16)
    slot_gates = jnp.sum(jnp.where(route_maps[0], route_gates[:, 0][:, None], 0.0), axis=0)
    slot_gates = slot_gates.reshape(experts, capacity)

    def place_rows(values):
        placed = jnp.einsum("ts,tc->sc", chosen, values, preferred_element_type=jnp.float32)
        return placed.astype(jnp.bfloat16).reshape(experts, capacity, values.shape[1])

    sent_inputs = place_rows(tokens)
    sent_grads = place_rows(cotangent)
    got_inputs, got_grads, got_gates = (
        lax.all_to_all(sent_inputs, "ep", split_axis=0, concat_axis=0, tiled=True),
        lax.all_to_all(sent_grads, "ep", split_axis=0, concat_axis=0, tiled=True),
        lax.all_to_all(
            slot_gates.astype(jnp.bfloat16), "ep", split_axis=0, concat_axis=0, tiled=True
        ).astype(slot_gates.dtype),
    )
    slot_inputs, slot_grads = (
        lax.all_gather(got_inputs, "ctx", axis=2, tiled=True),
        lax.all_gather(got_grads, "ctx", axis=2, tiled=True),
    )
    width = slot_inputs.shape[2]
    rows_in = slot_inputs.reshape(slot_count, width)
    grads_in = slot_grads.reshape(slot_count, width)
    gate_column = got_gates.reshape(slot_count, 1)
    gate_w = w_gate[0]
    up_w = w_up[0]
    down_w = w_down[0]
    pre_gate = jnp.dot(rows_in, gate_w, preferred_element_type=jnp.float32)
    pre_up = jnp.dot(rows_in, up_w, preferred_element_type=jnp.float32)
    sigma = jax.nn.sigmoid(pre_gate)
    activated = pre_gate * sigma
    hidden = (activated * pre_up).astype(jnp.bfloat16)
    partial_out = jnp.dot(hidden, down_w, preferred_element_type=jnp.float32).reshape(
        experts, capacity, width
    )
    expert_out = lax.psum_scatter(
        partial_out.astype(jnp.bfloat16), "ctx", scatter_dimension=2, tiled=True
    )
    contract_last = (((1,), (1,)), ((), ()))
    hidden_grad = gate_column * lax.dot_general(
        grads_in, down_w, contract_last, preferred_element_type=jnp.float32
    )
    grad_gate = (hidden_grad * pre_up * sigma * (1.0 + pre_gate * (1.0 - sigma))).astype(
        jnp.bfloat16
    )
    grad_up = (hidden_grad * activated).astype(jnp.bfloat16)
    contract_first = (((0,), (0,)), ((), ()))
    w_gate_grad = lax.dot_general(
        rows_in, grad_gate, contract_first, preferred_element_type=jnp.float32
    ).astype(jnp.bfloat16)[None]
    w_up_grad = lax.dot_general(
        rows_in, grad_up, contract_first, preferred_element_type=jnp.float32
    ).astype(jnp.bfloat16)[None]
    back_out = lax.all_to_all(expert_out, "ep", split_axis=0, concat_axis=0, tiled=True)
    back_terms = lax.dot_general(
        grad_gate, gate_w, contract_last, preferred_element_type=jnp.float32
    )
    back_terms = back_terms + lax.dot_general(
        grad_up, up_w, contract_last, preferred_element_type=jnp.float32
    )
    summed = lax.psum_scatter(
        back_terms.reshape(experts, capacity, width).astype(jnp.bfloat16),
        "ctx",
        scatter_dimension=2,
        tiled=True,
    )
    back_grad = lax.all_to_all(summed, "ep", split_axis=0, concat_axis=0, tiled=True)
    out_rows = back_out.reshape(slot_count, col_width)
    grad_rows = back_grad.reshape(slot_count, col_width)
    cotangent_wide = cotangent.astype(jnp.float32)
    route_matrix = route_maps[0].astype(jnp.bfloat16)
    picked = jnp.dot(route_matrix, out_rows, preferred_element_type=jnp.float32)
    layer_out = route_gates[:, 0][:, None] * picked
    gate_terms = [jnp.sum(picked * cotangent_wide, axis=1)]
    input_grad = jnp.dot(route_matrix, grad_rows, preferred_element_type=jnp.float32)
    gate_grad = lax.psum(jnp.stack(gate_terms, axis=1), "ctx")
    return (
        layer_out.astype(jnp.bfloat16),
        input_grad.astype(jnp.bfloat16),
        gate_grad,
        w_gate_grad,
        w_up_grad,
    )


def solution(mesh):
    in_specs = (
        P("ep", "ctx"),
        P("ep", "ctx"),
        P("ep", None),
        P("ep", None),
        P("ep", None, "ctx"),
        P("ep", None, "ctx"),
        P("ep", "ctx", None),
    )
    out_specs = (
        P("ep", "ctx"),
        P("ep", "ctx"),
        P("ep", None),
        P("ep", None, "ctx"),
        P("ep", None, "ctx"),
    )
    return jax.shard_map(shards, mesh=mesh, in_specs=in_specs, out_specs=out_specs, check_vma=False)
```

profile of v0, /device:TPU:0, one launch (start us, length us, event | category | flops | bytes accessed | tf_op | source)
XLA Modules:
  0.0 184.7 jit_solution(12868758092519926794)
XLA Ops:
  7.2 0.0 copy-start
  7.2 0.0 copy-start.9
  7.2 0.0 all-gather.3.cloned.1.call-start
  7.2 0.8 fusion.18
  8.0 0.2 reduce_window_sum.11
  8.2 0.8 select_reduce_fusion.1
  9.0 0.7 fusion.23
  9.7 0.0 copy-done
  9.7 0.3 convolution_convert_fusion.4
  10.0 18.3 %all_to_all.26 = bf16[8,24,896]{2,1,0:T(8,128)(2,1)} all-to-all(bf16[8,24,896]{2,1,0:T(8,128)(2,1)S(1)} %bitcast.69), channel_id=1, replica_groups=mesh['ctx'=4,'ep'=8] {'ep'}, dimensions={0} | all-to-all | bytes 688128 | tf_op jit(solution)/shard_map/all_to_all | solution.py:37
  28.3 0.0 all-gather.3.cloned.1.call-update
  28.3 0.0 all-gather.5.cloned.1.call-start
  28.4 1.2 convolution_convert_fusion.3
  29.6 14.0 %all_to_all.27 = bf16[8,24,896]{2,1,0:T(8,128)(2,1)} all-to-all(bf16[8,24,896]{2,1,0:T(8,128)(2,1)S(1)} %bitcast.70), channel_id=1, replica_groups=mesh['ctx'=4,'ep'=8] {'ep'}, dimensions={0} | all-to-all | bytes 688128 | tf_op jit(solution)/shard_map/all_to_all | solution.py:38
  43.6 0.0 all-gather.5.cloned.1.call-update
  43.7 0.0 reduce-scatter.7.cloned.1.call-start
  43.7 0.0 copy-done.9
  43.7 0.1 select_reduce_fusion
  43.8 0.1 convert_element_type.86
  43.9 9.3 %all_to_all.28 = bf16[8,1,24]{2,1,0:T(2,128)(2,1)S(1)} all-to-all(bf16[8,1,24]{2,1,0:T(2,128)(2,1)S(1)} %convert_element_type.86), channel_id=1, replica_groups=mesh['ctx'=4,'ep'=8] {'ep'}, dimensions={0} | all-to-all | bytes 768 | tf_op jit(solution)/shard_map/all_to_all | solution.py:39
  53.2 0.1 reshape.62
  53.3 0.0 all-gather.3.cloned.1.call-done
  53.3 0.0 copy-start.1
  53.3 0.0 copy-start.3
  53.3 3.8 %fusion.11 = f32[192,512]{1,0:T(8,128)S(1)} fusion(bf16[192,3584]{1,0:T(8,128)(2,1)} %bitcast.63, bf16[1,3584,512]{2,1,0:T(8,128)(2,1)} %param.11), kind=kOutput, calls=%fused_computation.15 | convolution fusion | flops 704643072 | bytes 5439488 | tf_op jit(solution)/shard_map/dot_general | solution.py:54
  57.1 0.1 copy-done.1
  57.2 0.4 copy-done.3
  57.6 0.9 fusion.7
  58.4 7.3 %all-gather.5.cloned.1.call-done = bf16[8,24,3584]{2,1,0:T(8,128)(2,1)} async-done(((bf16[8,24,896]{2,1,0:T(8,128)(2,1)}), bf16[8,24,3584]{2,1,0:T(8,128)(2,1)}) %all-gather.5.cloned.1.call-update) | async-done | bytes 1376272 | tf_op jit(solution)/shard_map/all_gather | solution.py:45
  65.7 4.0 %multiply_convert_fusion.1 = (bf16[192,512]{1,0:T(8,128)(2,1)S(1)}, bf16[192,512]{1,0:T(8,128)(2,1)S(1)}, bf16[192,512]{1,0:T(8,128)(2,1)S(1)}) fusion(f32[192,512]{1,0:T(8,128)S(1)} %fusion.11, f32[192,512]{1,0:T(8,128)S(1)} %fusion.7, bf16[192,3584]{1,0:T(8,128)(2,1)} %bitcast.77, bf16[1,512,3584]{2,1,0:T(8,128)(2,1)} %param.13, f32[192]{0:T(256)S(1)} %reshape.62), kind=kOutput, calls=%fused_computation.23 | convolution fusion | flops 706215936 | bytes 6423296 | tf_op jit(solution)/shard_map/dot_general | solution.py:66
  69.8 0.0 copy-start.6
  69.8 0.0 copy-start.7
  69.8 0.0 copy-done.4
  69.8 0.9 convolution_convert_fusion.2
  70.7 6.4 %copy.14 = bf16[8,24,3584]{1,0,2:T(8,128)(2,1)} copy(bf16[8,24,3584]{2,1,0:T(8,128)(2,1)S(1)} %convolution_convert_fusion.2) | data formatting | bytes 2752512
  77.1 9.6 %reshape.64 = bf16[3584,192]{1,0:T(8,128)(2,1)} reshape(bf16[3584,8,24]{2,1,0:T(8,128)(2,1)} %bitcast.59) | data formatting | bytes 2752512
  86.7 0.0 reduce-scatter.7.cloned.1.call-update
  86.7 0.0 reduce-scatter.9.cloned.1.call-start
  86.8 0.0 copy-done.6
  86.8 0.0 copy-start.2
  86.8 3.5 %fusion.9 = f32[192,3584]{1,0:T(8,128)S(1)} fusion(bf16[192,512]{1,0:T(8,128)(2,1)S(1)} %get-tuple-element.6, bf16[1,3584,512]{2,1,0:T(8,128)(2,1)} %param.11), kind=kOutput, calls=%fused_computation.13 | convolution fusion | flops 704643072 | bytes 6619136 | tf_op jit(solution)/shard_map/dot_general | solution.py:81
  90.3 0.0 copy-done.7
  90.3 0.0 copy-done.2
  90.4 1.3 fusion.2
  91.7 6.4 %copy.16 = bf16[8,24,3584]{1,0,2:T(8,128)(2,1)} copy(bf16[8,24,3584]{2,1,0:T(8,128)(2,1)S(1)} %bitcast.67) | data formatting | bytes 2752512
  98.1 9.6 %reshape.66 = bf16[3584,192]{1,0:T(8,128)(2,1)} reshape(bf16[3584,8,24]{2,1,0:T(8,128)(2,1)} %bitcast.60) | data formatting | bytes 2752512
  107.7 0.0 reduce-scatter.9.cloned.1.call-update
  107.7 9.0 %reduce-scatter.7.cloned.1.call-done = bf16[896,192]{1,0:T(8,128)(2,1)} async-done(((bf16[3584,192]{1,0:T(8,128)(2,1)}), bf16[896,192]{1,0:T(8,128)(2,1)}) %reduce-scatter.7.cloned.1.call-update) | async-done | bytes 344080
  116.7 2.6 %reshape.65 = bf16[896,8,24]{2,1,0:T(8,128)(2,1)S(1)} reshape(bf16[896,192]{1,0:T(8,128)(2,1)} %reduce-scatter.7.cloned.1.call-done) | data formatting | bytes 688128
  119.3 2.4 %copy.15 = bf16[8,24,896]{2,1,0:T(8,128)(2,1)} copy(bf16[8,24,896]{1,0,2:T(8,128)(2,1)S(1)} %bitcast.61) | data formatting | bytes 688128
  121.6 5.5 %all-to-all-start.1 = ((bf16[8,24,896]{2,1,0:T(8,128)(2,1)}), bf16[8,24,896]{2,1,0:T(8,128)(2,1)}, u32[]{:S(2)}, u32[]{:S(2)}) async-start(bf16[8,24,896]{2,1,0:T(8,128)(2,1)} %copy.15), calls=%async_computation.1 | async-start | bytes 688128 | tf_op jit(solution)/shard_map/all_to_all | solution.py:80
  127.1 22.6 %reduce-scatter.9.cloned.1.call-done = bf16[896,192]{1,0:T(8,128)(2,1)} async-done(((bf16[3584,192]{1,0:T(8,128)(2,1)}), bf16[896,192]{1,0:T(8,128)(2,1)}) %reduce-scatter.9.cloned.1.call-update) | async-done | bytes 344080
  149.7 2.6 %reshape.67 = bf16[896,8,24]{2,1,0:T(8,128)(2,1)S(1)} reshape(bf16[896,192]{1,0:T(8,128)(2,1)} %reduce-scatter.9.cloned.1.call-done) | data formatting | bytes 688128
  152.2 2.4 %copy.17 = bf16[8,24,896]{2,1,0:T(8,128)(2,1)} copy(bf16[8,24,896]{1,0,2:T(8,128)(2,1)S(1)} %bitcast.62) | data formatting | bytes 688128
  154.6 0.0 all-to-all-done.1
  154.6 5.5 %all-to-all-start.4 = ((bf16[8,24,896]{2,1,0:T(8,128)(2,1)}), bf16[8,24,896]{2,1,0:T(8,128)(2,1)S(1)}, u32[]{:S(2)}, u32[]{:S(2)}) async-start(bf16[8,24,896]{2,1,0:T(8,128)(2,1)} %copy.17), calls=%async_computation.4 | async-start | bytes 688128 | tf_op jit(solution)/shard_map/all_to_all | solution.py:93
  160.1 4.0 %fusion = bf16[1,3584,512]{2,1,0:T(8,128)(2,1)} fusion(bf16[192,3584]{1,0:T(8,128)(2,1)S(1)} %bitcast.65, bf16[192,512]{1,0:T(8,128)(2,1)} %copy-done.6), kind=kOutput, calls=%fused_computation.2 | convolution fusion | flops 706478080 | bytes 5242880 | tf_op jit(solution)/shard_map/dot_general | solution.py:74
  164.1 0.0 copy-done.8
  164.1 3.0 %fusion.1 = bf16[1,3584,512]{2,1,0:T(8,128)(2,1)} fusion(bf16[192,3584]{1,0:T(8,128)(2,1)S(1)} %bitcast.66, bf16[192,512]{1,0:T(8,128)(2,1)S(1)} %copy-done.8), kind=kOutput, calls=%fused_computation.3 | convolution fusion | flops 706478080 | bytes 5242880 | tf_op jit(solution)/shard_map/dot_general | solution.py:77
  167.1 0.0 copy-done.5
  167.1 2.0 %multiply_reduce_fusion = (f32[128]{0:T(128)S(1)}, bf16[128,896]{1,0:T(8,128)(2,1)}) fusion(bf16[128,896]{1,0:T(8,128)(2,1)S(1)} %copy-done.5, f32[128]{0:T(128)S(1)} %bitcast.75, bf16[192,896]{1,0:T(8,128)(2,1)} %bitcast.11, s32[128]{0:T(128)S(1)} %fusion.23), kind=kOutput, calls=%fused_computation.21 | convolution fusion | flops 44638080 | bytes 804352 | tf_op jit(solution)/shard_map/dot_general | solution.py:98
  169.1 1.6 all-to-all-done.4
  170.8 1.0 convolution_convert_fusion.5
  171.7 6.4 %psum.7 = f32[128,1]{0,1:T(1,128)} all-reduce(f32[128,1]{0,1:T(1,128)S(1)} %bitcast.76), channel_id=1, replica_groups=mesh['ctx'=4,'ep'=8] {'ctx'}, use_global_device_ids=true, to_apply=%region_6.7 | all-reduce | flops 128 | bytes 1024 | tf_op jit(solution)/shard_map/psum | solution.py:102
  (4 shorter events, 0.0 us)
Async XLA Ops:
  7.2 2.5 %copy-start = (bf16[128,896]{1,0:T(8,128)(2,1)S(1)}, bf16[128,896]{1,0:T(8,128)(2,1)}, u32[]{:S(2)}) copy-start(bf16[128,896]{1,0:T(8,128)(2,1)} %param.7) | copy-start | bytes 688132
  7.2 36.5 %copy-start.9 = (f32[128,1]{0,1:T(1,128)S(1)}, f32[128,1]{0,1:T(1,128)}, u32[]{:S(2)}) copy-start(f32[128,1]{0,1:T(1,128)} %param.10) | copy-start | bytes 1540
  7.2 46.1 %all-gather.3.cloned.1.call-start = ((), (), s32[]{:S(2)}) async-start(), calls=%async_computation.7 | async-start | bytes 1720320 | tf_op jit(solution)/shard_map/all_gather | solution.py:44
  28.3 37.4 %all-gather.5.cloned.1.call-start = ((), (), s32[]{:S(2)}) async-start(), calls=%async_computation.8 | async-start | bytes 1720320 | tf_op jit(solution)/shard_map/all_gather | solution.py:45
  43.7 73.0 %reduce-scatter.7.cloned.1.call-start = ((), (), s32[]{:S(2)}) async-start(), calls=%async_computation.9 | async-start | bytes 2293760
  53.3 3.9 %copy-start.1 = (bf16[1,3584,512]{2,1,0:T(8,128)(2,1)S(1)}, bf16[1,3584,512]{2,1,0:T(8,128)(2,1)}, u32[]{:S(2)}) copy-start(bf16[1,3584,512]{2,1,0:T(8,128)(2,1)} %param.12) | copy-start | bytes 11010052
  53.3 4.3 %copy-start.3 = (bf16[8,24,3584]{2,1,0:T(8,128)(2,1)S(1)}, bf16[8,24,3584]{2,1,0:T(8,128)(2,1)}, u32[]{:S(2)}) copy-start(bf16[8,24,3584]{2,1,0:T(8,128)(2,1)} %all-gather.3.cloned.1.call-done) | copy-start | bytes 4128772
  65.7 4.1 %copy-start.4 = (bf16[1,512,3584]{2,1,0:T(8,128)(2,1)S(1)}, bf16[1,512,3584]{2,1,0:T(8,128)(2,1)}, u32[]{:S(2)}) copy-start(bf16[1,512,3584]{2,1,0:T(8,128)(2,1)} %param.13) | copy-start | bytes 11010052
  69.8 17.0 %copy-start.6 = (bf16[192,512]{1,0:T(8,128)(2,1)}, bf16[192,512]{1,0:T(8,128)(2,1)S(1)}, u32[]{:S(2)}) copy-start(bf16[192,512]{1,0:T(8,128)(2,1)S(1)} %get-tuple-element.6) | copy-start | bytes 589828
  69.8 20.6 %copy-start.7 = (bf16[192,512]{1,0:T(8,128)(2,1)}, bf16[192,512]{1,0:T(8,128)(2,1)S(1)}, u32[]{:S(2)}) copy-start(bf16[192,512]{1,0:T(8,128)(2,1)S(1)} %get-tuple-element.5) | copy-start | bytes 589828
  86.7 62.9 %reduce-scatter.9.cloned.1.call-start = ((), (), s32[]{:S(2)}) async-start(), calls=%async_computation.10 | async-start | bytes 2293760
  86.8 3.6 %copy-start.2 = (bf16[1,3584,512]{2,1,0:T(8,128)(2,1)S(1)}, bf16[1,3584,512]{2,1,0:T(8,128)(2,1)}, u32[]{:S(2)}) copy-start(bf16[1,3584,512]{2,1,0:T(8,128)(2,1)} %param.12) | copy-start | bytes 11010052
  121.6 33.0 %all-to-all-start.1 = ((bf16[8,24,896]{2,1,0:T(8,128)(2,1)}), bf16[8,24,896]{2,1,0:T(8,128)(2,1)}, u32[]{:S(2)}, u32[]{:S(2)}) async-start(bf16[8,24,896]{2,1,0:T(8,128)(2,1)} %copy.15), calls=%async_computation.1 | async-start | bytes 688128 | tf_op jit(solution)/shard_map/all_to_all | solution.py:80
  154.6 16.2 %all-to-all-start.4 = ((bf16[8,24,896]{2,1,0:T(8,128)(2,1)}), bf16[8,24,896]{2,1,0:T(8,128)(2,1)S(1)}, u32[]{:S(2)}, u32[]{:S(2)}) async-start(bf16[8,24,896]{2,1,0:T(8,128)(2,1)} %copy.17), calls=%async_computation.4 | async-start | bytes 688128 | tf_op jit(solution)/shard_map/all_to_all | solution.py:93
  160.1 4.0 %copy-start.8 = (bf16[192,512]{1,0:T(8,128)(2,1)S(1)}, bf16[192,512]{1,0:T(8,128)(2,1)}, u32[]{:S(2)}) copy-start(bf16[192,512]{1,0:T(8,128)(2,1)} %copy-done.7) | copy-start | bytes 589828
  164.1 3.0 %copy-start.5 = (bf16[128,896]{1,0:T(8,128)(2,1)S(1)}, bf16[128,896]{1,0:T(8,128)(2,1)}, u32[]{:S(2)}) copy-start(bf16[128,896]{1,0:T(8,128)(2,1)} %param.8) | copy-start | bytes 688132
Sparse Core Ops, SparseCore 0:
  28.5 17.0 all-gather.2
  47.1 18.5 all-gather.4
  86.8 29.7 reduce-scatter.6
  119.8 29.8 reduce-scatter.8
where the time goes:
time: 186 us; the launch traced here: 185 us
  blocking collectives  48.1 us (26%)
  local copies, waits for them, and re-layouts  42.5 us (23%)
  waiting for transfers between devices  40.5 us (22%)
  matrix products  25.9 us (14%)
  between operations  13.9 us (7%)
  starting transfers between devices  11.2 us (6%)
  other arithmetic  2.59 us (1%)
    unnamed x28, local copies, waits for them, and re-layouts  42.3 us
    unnamed x6, waiting for transfers between devices  31.6 us
    all_to_all x1, blocking collectives, shards(): lax.all_to_all(sent_inputs, 'ep', split_axis=0, concat_axis=0, tiled=True)  18.3 us
    all_to_all x1, blocking collectives, shards(): lax.all_to_all(sent_grads, 'ep', split_axis=0, concat_axis=0, tiled=True)  14 us
    all_to_all x1, blocking collectives, shards(): lax.all_to_all(slot_gates.astype(jnp.bfloat16), 'ep', split_axis=0, conca...  9.28 us
    all_gather x1, waiting for transfers between devices, shards(): lax.all_gather(got_grads, 'ctx', axis=2, tiled=True)  7.28 us
    psum x1, blocking collectives, shards(): gate_grad = lax.psum(jnp.stack(gate_terms, axis=1), 'ctx')  6.42 us
    all_to_all x1, starting transfers between devices, shards(): lax.all_to_all(expert_out, 'ep', split_axis=0, concat_axis=0, tiled=True)  5.51 us
  transfers between devices with their start and end apart: 6, of which 4 were waited for; matrix products, arithmetic and copies ran while one was open for 25% of the time, Pallas kernels for 0%

commit v1 on v0

--- a/solution.py
+++ b/solution.py
@@ -2,6 +2,22 @@
 import jax.numpy as jnp
 from jax import lax
 from jax.sharding import PartitionSpec as P
+
+
+def swapped_with_each(x, axis, split, join):
+    ways, here = (lax.axis_size(axis), lax.axis_index(axis))
+    width = x.shape[split] // ways
+    dims = list(x.shape)
+    dims[split] = width
+    height = dims[join]
+    dims[join] = height * ways
+    full = jnp.zeros(dims, x.dtype)
+    for mask in range(ways):
+        part = lax.dynamic_slice_in_dim(x, (here ^ mask) * width, width, axis=split)
+        if mask:
+            part = lax.ppermute(part, axis, [(d, d ^ mask) for d in range(ways)])
+        full = lax.dynamic_update_slice_in_dim(full, part, (here ^ mask) * height, axis=join)
+    return full
 
 
 def route_tables(expert_ids, experts, capacity):
@@ -77,7 +93,7 @@
     w_up_grad = lax.dot_general(
         rows_in, grad_up, contract_first, preferred_element_type=jnp.float32
     ).astype(jnp.bfloat16)[None]
-    back_out = lax.all_to_all(expert_out, "ep", split_axis=0, concat_axis=0, tiled=True)
+    back_out = swapped_with_each(expert_out, "ep", 0, 0)
     back_terms = lax.dot_general(
         grad_gate, gate_w, contract_last, preferred_element_type=jnp.float32
     )

time: 186 us -> 188 us (1.011)
  waiting for transfers between devices: 40.5 us -> 21.9 us
  local copies, waits for them, and re-layouts: 42.5 us -> 57.9 us
  starting transfers between devices: 11.2 us -> 18.6 us
  matrix products: 25.9 us -> 23.9 us
    unnamed x6, waiting for transfers between devices: 31.6 us -> 10 us
    ppermute x0 -> x7, starting transfers between devices: none -> 12.7 us  [swapped_with_each(): part = lax.ppermute(part, axis, [(d, d ^ mask) for d in range(ways)])]
    unnamed x28 -> x29, local copies, waits for them, and re-layouts: 42.3 us -> 50.5 us
    all_to_all x1 -> x0, starting transfers between devices: 5.51 us -> none  [shards(): lax.all_to_all(expert_out, 'ep', split_axis=0, concat_axis=0, tiled=True)]
    dynamic_slice x0 -> x1, local copies, waits for them, and re-layouts: none -> 4.75 us  [swapped_with_each(): part = lax.dynamic_slice_in_dim(x, (here ^ mask) * width, width, axis=split)]
    ppermute x0 -> x7, waiting for transfers between devices: none -> 4.57 us  [swapped_with_each(): part = lax.ppermute(part, axis, [(d, d ^ mask) for d in range(ways)])]
    dynamic_update_slice x0 -> x8, local copies, waits for them, and re-layouts: none -> 2.46 us  [swapped_with_each(): lax.dynamic_update_slice_in_dim(full, part, (here ^ mask) * height, axis=...]
  transfers between devices with their start and end apart: 6 -> 12, of which waited for: 4 -> 5; matrix products, arithmetic and copies ran while one was open for 25% -> 32% of each run, Pallas kernels for 0% -> 0%
where the time goes in v1:
time: 188 us; the launch traced here: 187 us
  local copies, waits for them, and re-layouts  57.9 us (31%)
  blocking collectives  48.1 us (26%)
  matrix products  23.9 us (13%)
  waiting for transfers between devices  21.9 us (12%)
  starting transfers between devices  18.6 us (10%)
  between operations  14 us (7%)
  other arithmetic  2.59 us (1%)
    unnamed x29, local copies, waits for them, and re-layouts  50.5 us
    all_to_all x1, blocking collectives, shards(): lax.all_to_all(sent_inputs, 'ep', split_axis=0, concat_axis=0, tiled=True)  18.4 us
    all_to_all x1, blocking collectives, shards(): lax.all_to_all(sent_grads, 'ep', split_axis=0, concat_axis=0, tiled=True)  14 us
    ppermute x7, starting transfers between devices, swapped_with_each(): part = lax.ppermute(part, axis, [(d, d ^ mask) for d in range(ways)])  12.7 us
    unnamed x6, waiting for transfers between devices  10 us
    all_to_all x1, blocking collectives, shards(): lax.all_to_all(slot_gates.astype(jnp.bfloat16), 'ep', split_axis=0, conca...  9.28 us
    all_gather x1, waiting for transfers between devices, shards(): lax.all_gather(got_grads, 'ctx', axis=2, tiled=True)  7.29 us
    psum x1, blocking collectives, shards(): gate_grad = lax.psum(jnp.stack(gate_terms, axis=1), 'ctx')  6.4 us
  transfers between devices with their start and end apart: 12, of which 5 were waited for; matrix products, arithmetic and copies ran while one was open for 32% of the time, Pallas kernels for 0%

profile of v1, /device:TPU:0, one launch (start us, length us, event | category | flops | bytes accessed | tf_op | source)
XLA Modules:
  0.0 186.9 jit_solution(9131441421881764725)
XLA Ops:
  7.2 0.0 all-gather.3.cloned.1.call-start
  7.2 0.8 fusion.18
  8.0 0.2 reduce_window_sum.11
  8.2 0.8 select_reduce_fusion.1
  9.0 0.7 fusion.23
  9.7 0.3 convolution_convert_fusion.4
  10.0 18.4 %all_to_all.21 = bf16[8,24,896]{2,1,0:T(8,128)(2,1)} all-to-all(bf16[8,24,896]{2,1,0:T(8,128)(2,1)S(1)} %bitcast.70), channel_id=1, replica_groups=mesh['ctx'=4,'ep'=8] {'ep'}, dimensions={0} | all-to-all | bytes 688128 | tf_op jit(solution)/shard_map/all_to_all | solution.py:53
  28.3 0.0 all-gather.3.cloned.1.call-update
  28.3 0.0 all-gather.5.cloned.1.call-start
  28.4 1.2 convolution_convert_fusion.3
  29.6 14.0 %all_to_all.22 = bf16[8,24,896]{2,1,0:T(8,128)(2,1)} all-to-all(bf16[8,24,896]{2,1,0:T(8,128)(2,1)S(1)} %bitcast.71), channel_id=1, replica_groups=mesh['ctx'=4,'ep'=8] {'ep'}, dimensions={0} | all-to-all | bytes 688128 | tf_op jit(solution)/shard_map/all_to_all | solution.py:54
  43.6 0.0 all-gather.5.cloned.1.call-update
  43.7 0.0 reduce-scatter.7.cloned.1.call-start
  43.7 0.1 select_reduce_fusion
  43.8 0.1 convert_element_type.86
  43.9 9.3 %all_to_all.23 = bf16[8,1,24]{2,1,0:T(2,128)(2,1)S(1)} all-to-all(bf16[8,1,24]{2,1,0:T(2,128)(2,1)S(1)} %convert_element_type.86), channel_id=1, replica_groups=mesh['ctx'=4,'ep'=8] {'ep'}, dimensions={0} | all-to-all | bytes 768 | tf_op jit(solution)/shard_map/all_to_all | solution.py:55
  53.2 0.1 reshape.62
  53.3 3.8 %fusion.11 = f32[192,512]{1,0:T(8,128)S(1)} fusion(bf16[192,3584]{1,0:T(8,128)(2,1)} %bitcast.63, bf16[1,3584,512]{2,1,0:T(8,128)(2,1)} %param.11), kind=kOutput, calls=%fused_computation.15 | convolution fusion | flops 704643072 | bytes 5439488 | tf_op jit(solution)/shard_map/dot_general | solution.py:70
  57.1 0.1 copy-done.1
  57.2 0.4 copy-done.3
  57.6 0.9 fusion.7
  58.4 7.3 %all-gather.5.cloned.1.call-done = bf16[8,24,3584]{2,1,0:T(8,128)(2,1)} async-done(((bf16[8,24,896]{2,1,0:T(8,128)(2,1)}), bf16[8,24,3584]{2,1,0:T(8,128)(2,1)}) %all-gather.5.cloned.1.call-update) | async-done | bytes 1376272 | tf_op jit(solution)/shard_map/all_gather | solution.py:61
  65.7 4.0 %multiply_convert_fusion.1 = (bf16[192,512]{1,0:T(8,128)(2,1)S(1)}, bf16[192,512]{1,0:T(8,128)(2,1)S(1)}, bf16[192,512]{1,0:T(8,128)(2,1)S(1)}) fusion(f32[192,512]{1,0:T(8,128)S(1)} %fusion.11, f32[192,512]{1,0:T(8,128)S(1)} %fusion.7, bf16[192,3584]{1,0:T(8,128)(2,1)} %bitcast.78, bf16[1,512,3584]{2,1,0:T(8,128)(2,1)} %param.13, f32[192]{0:T(256)S(1)} %reshape.62), kind=kOutput, calls=%fused_computation.23 | convolution fusion | flops 706215936 | bytes 6423296 | tf_op jit(solution)/shard_map/dot_general | solution.py:82
  69.8 0.9 convolution_convert_fusion.2
  70.7 6.3 %copy.14 = bf16[8,24,3584]{1,0,2:T(8,128)(2,1)} copy(bf16[8,24,3584]{2,1,0:T(8,128)(2,1)S(1)} %convolution_convert_fusion.2) | data formatting | bytes 2752512
  77.0 9.6 %reshape.64 = bf16[3584,192]{1,0:T(8,128)(2,1)} reshape(bf16[3584,8,24]{2,1,0:T(8,128)(2,1)} %bitcast.59) | data formatting | bytes 2752512
  86.6 0.0 reduce-scatter.7.cloned.1.call-update
  86.7 0.2 reduce-scatter.9.cloned.1.call-start
  86.9 3.5 %fusion.9 = f32[192,3584]{1,0:T(8,128)S(1)} fusion(bf16[192,512]{1,0:T(8,128)(2,1)S(1)} %get-tuple-element.14, bf16[1,3584,512]{2,1,0:T(8,128)(2,1)} %param.11), kind=kOutput, calls=%fused_computation.13 | convolution fusion | flops 704643072 | bytes 6619136 | tf_op jit(solution)/shard_map/dot_general | solution.py:97
  90.4 1.3 fusion.2
  91.8 6.3 %copy.16 = bf16[8,24,3584]{1,0,2:T(8,128)(2,1)} copy(bf16[8,24,3584]{2,1,0:T(8,128)(2,1)S(1)} %bitcast.67) | data formatting | bytes 2752512
  98.1 9.6 %reshape.66 = bf16[3584,192]{1,0:T(8,128)(2,1)} reshape(bf16[3584,8,24]{2,1,0:T(8,128)(2,1)} %bitcast.60) | data formatting | bytes 2752512
  107.8 3.0 %fusion = bf16[1,3584,512]{2,1,0:T(8,128)(2,1)} fusion(bf16[192,3584]{1,0:T(8,128)(2,1)S(1)} %bitcast.65, bf16[192,512]{1,0:T(8,128)(2,1)S(1)} %get-tuple-element.14), kind=kOutput, calls=%fused_computation.2 | convolution fusion | flops 706478080 | bytes 5242880 | tf_op jit(solution)/shard_map/dot_general | solution.py:90
  110.8 3.0 %fusion.1 = bf16[1,3584,512]{2,1,0:T(8,128)(2,1)} fusion(bf16[192,3584]{1,0:T(8,128)(2,1)S(1)} %bitcast.66, bf16[192,512]{1,0:T(8,128)(2,1)S(1)} %get-tuple-element.13), kind=kOutput, calls=%fused_computation.3 | convolution fusion | flops 706478080 | bytes 5242880 | tf_op jit(solution)/shard_map/dot_general | solution.py:93
  113.8 2.8 %reduce-scatter.7.cloned.1.call-done = bf16[896,192]{1,0:T(8,128)(2,1)} async-done(((bf16[3584,192]{1,0:T(8,128)(2,1)}), bf16[896,192]{1,0:T(8,128)(2,1)}) %reduce-scatter.7.cloned.1.call-update) | async-done | bytes 344080
  116.6 2.6 %reshape.65 = bf16[896,8,24]{2,1,0:T(8,128)(2,1)S(1)} reshape(bf16[896,192]{1,0:T(8,128)(2,1)} %reduce-scatter.7.cloned.1.call-done) | data formatting | bytes 688128
  119.2 4.8 %constant_dynamic-slice_fusion = (bf16[1,24,896]{1,0,2:T(2,128)(2,1)S(1)}, bf16[1,24,896]{1,0,2:T(2,128)(2,1)S(1)}, bf16[1,24,896]{1,0,2:T(2,128)(2,1)S(1)}, bf1...) fusion(bf16[8,24,896]{1,0,2:T(8,128)(2,1)S(1)} %bitcast.61, ...), kind=kLoop, calls=%fused_computation.39 | loop fusion | bytes 688160 | tf_op jit(solution)/shard_map/dynamic_slice | solution.py:16
  123.9 1.2 copy.18
  125.2 1.8 copy.19
  126.9 1.5 collective-permute-start
  128.4 1.8 copy.20
  130.2 1.5 collective-permute-start.1
  131.7 1.8 copy.21
  133.4 0.5 collective-permute-start.2
  134.0 1.8 copy.22
  135.7 2.4 %collective-permute-start.3 = (bf16[1,24,896]{2,1,0:T(8,128)(2,1)}, bf16[1,24,896]{2,1,0:T(8,128)(2,1)S(1)}, u32[]{:S(2)}, u32[]{:S(2)}) collective-permute-start(bf16[1,24,896]{2,1,0:T(8,128)(2,1)} %copy.22), channel_id=1, source_target_pairs={{0,4},{1,5},{2,6},{3,7},{4,0},{5,1},{6,2},{7,3},{8,12},{9,13},{10,... | collective-permute-start | bytes 129032 | tf_op jit(solution)/shard_map/ppermute | solution.py:18
  138.1 1.1 copy.23
  139.3 1.4 collective-permute-start.4
  140.7 0.6 copy.24
  141.3 0.6 copy.25
  141.9 7.1 %reduce-scatter.9.cloned.1.call-done = bf16[896,192]{1,0:T(8,128)(2,1)} async-done(((bf16[3584,192]{1,0:T(8,128)(2,1)}), bf16[896,192]{1,0:T(8,128)(2,1)}) %reduce-scatter.9.cloned.1.call-update) | async-done | bytes 344080
  149.0 2.6 %reshape.67 = bf16[896,8,24]{2,1,0:T(8,128)(2,1)S(1)} reshape(bf16[896,192]{1,0:T(8,128)(2,1)} %reduce-scatter.9.cloned.1.call-done) | data formatting | bytes 688128
  151.6 2.4 %copy.17 = bf16[8,24,896]{2,1,0:T(8,128)(2,1)} copy(bf16[8,24,896]{1,0,2:T(8,128)(2,1)S(1)} %bitcast.62) | data formatting | bytes 688128
  154.0 5.5 %all-to-all-start.3 = ((bf16[8,24,896]{2,1,0:T(8,128)(2,1)}), bf16[8,24,896]{2,1,0:T(8,128)(2,1)S(1)}, u32[]{:S(2)}, u32[]{:S(2)}) async-start(bf16[8,24,896]{2,1,0:T(8,128)(2,1)} %copy.17), calls=%async_computation.3 | async-start | bytes 688128 | tf_op jit(solution)/shard_map/all_to_all | solution.py:109
  159.5 3.9 %collective-permute-start.5 = (bf16[1,24,896]{2,1,0:T(8,128)(2,1)S(1)}, bf16[1,24,896]{2,1,0:T(8,128)(2,1)S(1)}, u32[]{:S(2)}, u32[]{:S(2)}) collective-permute-start(bf16[1,24,896]{2,1,0:T(8,128)(2,1)S(1)} %copy.24), channel_id=1, source_target_pairs={{0,6},{1,7},{2,4},{3,5},{4,2},{5,3},{6,0},{7,1},{8,14},{9,15},{10,... | collective-permute-start | bytes 129032 | tf_op jit(solution)/shard_map/ppermute | solution.py:18
  163.4 0.8 constant_dynamic-update-slice_fusion.5
  164.2 1.5 collective-permute-start.6
  165.7 0.8 constant_dynamic-update-slice_fusion.4
  166.5 0.8 constant_dynamic-update-slice_fusion.3
  167.4 3.2 %collective-permute-done.5 = bf16[1,24,896]{2,1,0:T(8,128)(2,1)S(1)} collective-permute-done((bf16[1,24,896]{2,1,0:T(8,128)(2,1)S(1)}, bf16[1,24,896]{2,1,0:T(8,128)(2,1)S(1)}, u32[]{:S(2)}, u32[]{:S(2)}) %collective-permute-start.5) | collective-permute-done | bytes 43040 | tf_op jit(solution)/shard_map/ppermute | solution.py:18
  170.6 1.4 collective-permute-done.6
  171.9 1.1 multiply_reduce_fusion
  173.0 6.4 %psum.7 = f32[128,1]{0,1:T(1,128)} all-reduce(f32[128,1]{0,1:T(1,128)S(1)} %bitcast.77), channel_id=1, replica_groups=mesh['ctx'=4,'ep'=8] {'ctx'}, use_global_device_ids=true, to_apply=%region_6.7 | all-reduce | flops 128 | bytes 1024 | tf_op jit(solution)/shard_map/psum | solution.py:118
  179.4 1.0 convolution_convert_fusion.5
  (27 shorter events, 0.2 us)
Async XLA Ops:
  7.2 2.5 %copy-start = (bf16[128,896]{1,0:T(8,128)(2,1)S(1)}, bf16[128,896]{1,0:T(8,128)(2,1)}, u32[]{:S(2)}) copy-start(bf16[128,896]{1,0:T(8,128)(2,1)} %param.7) | copy-start | bytes 688132
  7.2 36.5 %copy-start.6 = (f32[128,1]{0,1:T(1,128)S(1)}, f32[128,1]{0,1:T(1,128)}, u32[]{:S(2)}) copy-start(f32[128,1]{0,1:T(1,128)} %param.10) | copy-start | bytes 1540
  7.2 46.1 %all-gather.3.cloned.1.call-start = ((), (), s32[]{:S(2)}) async-start(), calls=%async_computation.6 | async-start | bytes 1720320 | tf_op jit(solution)/shard_map/all_gather | solution.py:60
  28.3 37.4 %all-gather.5.cloned.1.call-start = ((), (), s32[]{:S(2)}) async-start(), calls=%async_computation.7 | async-start | bytes 1720320 | tf_op jit(solution)/shard_map/all_gather | solution.py:61
  43.7 73.0 %reduce-scatter.7.cloned.1.call-start = ((), (), s32[]{:S(2)}) async-start(), calls=%async_computation.8 | async-start | bytes 2293760
  53.3 3.9 %copy-start.1 = (bf16[1,3584,512]{2,1,0:T(8,128)(2,1)S(1)}, bf16[1,3584,512]{2,1,0:T(8,128)(2,1)}, u32[]{:S(2)}) copy-start(bf16[1,3584,512]{2,1,0:T(8,128)(2,1)} %param.12) | copy-start | bytes 11010052
  53.3 4.3 %copy-start.3 = (bf16[8,24,3584]{2,1,0:T(8,128)(2,1)S(1)}, bf16[8,24,3584]{2,1,0:T(8,128)(2,1)}, u32[]{:S(2)}) copy-start(bf16[8,24,3584]{2,1,0:T(8,128)(2,1)} %all-gather.3.cloned.1.call-done) | copy-start | bytes 4128772
  65.7 4.0 %copy-start.4 = (bf16[1,512,3584]{2,1,0:T(8,128)(2,1)S(1)}, bf16[1,512,3584]{2,1,0:T(8,128)(2,1)}, u32[]{:S(2)}) copy-start(bf16[1,512,3584]{2,1,0:T(8,128)(2,1)} %param.13) | copy-start | bytes 11010052
  86.7 62.4 %reduce-scatter.9.cloned.1.call-start = ((), (), s32[]{:S(2)}) async-start(), calls=%async_computation.9 | async-start | bytes 2293760
  86.9 3.5 %copy-start.2 = (bf16[1,3584,512]{2,1,0:T(8,128)(2,1)S(1)}, bf16[1,3584,512]{2,1,0:T(8,128)(2,1)}, u32[]{:S(2)}) copy-start(bf16[1,3584,512]{2,1,0:T(8,128)(2,1)} %param.12) | copy-start | bytes 11010052
  126.9 32.6 %collective-permute-start = (bf16[1,24,896]{2,1,0:T(8,128)(2,1)}, bf16[1,24,896]{2,1,0:T(8,128)(2,1)}, u32[]{:S(2)}, u32[]{:S(2)}) collective-permute-start(bf16[1,24,896]{2,1,0:T(8,128)(2,1)} %copy.19), channel_id=1, source_target_pairs={{0,1},{1,0},{2,3},{3,2},{4,5},{5,4},{6,7},{7,6},{8,9},{9,8},{10,11... | collective-permute-start | bytes 129032 | tf_op jit(solution)/shard_map/ppermute | solution.py:18
  130.2 34.0 %collective-permute-start.1 = (bf16[1,24,896]{2,1,0:T(8,128)(2,1)}, bf16[1,24,896]{2,1,0:T(8,128)(2,1)}, u32[]{:S(2)}, u32[]{:S(2)}) collective-permute-start(bf16[1,24,896]{2,1,0:T(8,128)(2,1)} %copy.20), channel_id=1, source_target_pairs={{0,2},{1,3},{2,0},{3,1},{4,6},{5,7},{6,4},{7,5},{8,10},{9,11},{10,... | collective-permute-start | bytes 129032 | tf_op jit(solution)/shard_map/ppermute | solution.py:18
  133.4 33.1 %collective-permute-start.2 = (bf16[1,24,896]{2,1,0:T(8,128)(2,1)}, bf16[1,24,896]{2,1,0:T(8,128)(2,1)}, u32[]{:S(2)}, u32[]{:S(2)}) collective-permute-start(bf16[1,24,896]{2,1,0:T(8,128)(2,1)} %copy.21), channel_id=1, source_target_pairs={{0,3},{1,2},{2,1},{3,0},{4,7},{5,6},{6,5},{7,4},{8,11},{9,10},{10,... | collective-permute-start | bytes 129032 | tf_op jit(solution)/shard_map/ppermute | solution.py:18
  135.7 31.6 %collective-permute-start.3 = (bf16[1,24,896]{2,1,0:T(8,128)(2,1)}, bf16[1,24,896]{2,1,0:T(8,128)(2,1)S(1)}, u32[]{:S(2)}, u32[]{:S(2)}) collective-permute-start(bf16[1,24,896]{2,1,0:T(8,128)(2,1)} %copy.22), channel_id=1, source_target_pairs={{0,4},{1,5},{2,6},{3,7},{4,0},{5,1},{6,2},{7,3},{8,12},{9,13},{10,... | collective-permute-start | bytes 129032 | tf_op jit(solution)/shard_map/ppermute | solution.py:18
  139.3 28.1 %collective-permute-start.4 = (bf16[1,24,896]{2,1,0:T(8,128)(2,1)}, bf16[1,24,896]{2,1,0:T(8,128)(2,1)S(1)}, u32[]{:S(2)}, u32[]{:S(2)}) collective-permute-start(bf16[1,24,896]{2,1,0:T(8,128)(2,1)} %copy.23), channel_id=1, source_target_pairs={{0,5},{1,4},{2,7},{3,6},{4,1},{5,0},{6,3},{7,2},{8,13},{9,12},{10,... | collective-permute-start | bytes 129032 | tf_op jit(solution)/shard_map/ppermute | solution.py:18
  141.9 30.1 %copy-start.5 = (bf16[128,896]{1,0:T(8,128)(2,1)S(1)}, bf16[128,896]{1,0:T(8,128)(2,1)}, u32[]{:S(2)}) copy-start(bf16[128,896]{1,0:T(8,128)(2,1)} %param.8) | copy-start | bytes 688132
  154.0 25.5 %all-to-all-start.3 = ((bf16[8,24,896]{2,1,0:T(8,128)(2,1)}), bf16[8,24,896]{2,1,0:T(8,128)(2,1)S(1)}, u32[]{:S(2)}, u32[]{:S(2)}) async-start(bf16[8,24,896]{2,1,0:T(8,128)(2,1)} %copy.17), calls=%async_computation.3 | async-start | bytes 688128 | tf_op jit(solution)/shard_map/all_to_all | solution.py:109
  159.5 11.1 %collective-permute-start.5 = (bf16[1,24,896]{2,1,0:T(8,128)(2,1)S(1)}, bf16[1,24,896]{2,1,0:T(8,128)(2,1)S(1)}, u32[]{:S(2)}, u32[]{:S(2)}) collective-permute-start(bf16[1,24,896]{2,1,0:T(8,128)(2,1)S(1)} %copy.24), channel_id=1, source_target_pairs={{0,6},{1,7},{2,4},{3,5},{4,2},{5,3},{6,0},{7,1},{8,14},{9,15},{10,... | collective-permute-start | bytes 129032 | tf_op jit(solution)/shard_map/ppermute | solution.py:18
  164.2 7.7 %collective-permute-start.6 = (bf16[1,24,896]{2,1,0:T(8,128)(2,1)S(1)}, bf16[1,24,896]{2,1,0:T(8,128)(2,1)S(1)}, u32[]{:S(2)}, u32[]{:S(2)}) collective-permute-start(bf16[1,24,896]{2,1,0:T(8,128)(2,1)S(1)} %copy.25), channel_id=1, source_target_pairs={{0,7},{1,6},{2,5},{3,4},{4,3},{5,2},{6,1},{7,0},{8,15},{9,14},{10,... | collective-permute-start | bytes 129032 | tf_op jit(solution)/shard_map/ppermute | solution.py:18
Sparse Core Ops, SparseCore 0:
  28.5 17.0 all-gather.2
  47.1 18.5 all-gather.4
  86.8 29.7 reduce-scatter.6
  119.2 29.8 reduce-scatter.8
